TPU v7x, 256 devices: a whole 4x4x8 slice. The times are simulated.
256 devices in a mesh: group: 32 (over x, z_lo, core), tp: 8 (over y, z_hi).
Axes of the slice: x: 4, y: 4, z: 8 (z_hi: 2, z_lo: 4; z = z_hi * 4 + z_lo), core: 2. Of those that a mesh axis runs over, the one named last changes fastest.
Arguments:
- prefill_x: bfloat16 [16384, 4096], P('group', 'tp'), may hold values from -6 to 6
- decode_x: bfloat16 [128, 4096], P('group', 'tp'), may hold values from -6 to 6
- ln_gain: float32 [4096], replicated, may hold values from 0.1 to 1.9
- ln_bias: float32 [4096], replicated, may hold values from -3 to 3
- qkv_weight: bfloat16 [4096, 3, 2048], P(None, None, 'tp'), may hold values from -0.09375 to 0.09375
- qkv_bias: float32 [3, 2048], P(None, 'tp'), may hold values from -3 to 3
- prior_cache: bfloat16 [32, 2, 512, 2048], P('group', None, None, 'tp'), may hold values from -144 to 144, as said below
- prefill_offset: int32 [32], P('group'), may hold values from 0 to 512, as said below
- home_cache: bfloat16 [128, 2, 256, 2048], P('group', None, None, 'tp'), may hold values from -144 to 144, as said below
- piece_len: int32 [128, 3], P('group'), may hold values from 0 to 1024, as said below
- side_store: bfloat16 [256, 2, 1024, 2048], P('group', None, None, 'tp'), may hold values from -144 to 144, as said below
Outputs:
- prefill_out: bfloat16 [16384, 2048], P('group', 'tp')
- decode_out: bfloat16 [128, 2048], P('group', 'tp')
Inputs may be any that keep to these rules, and one draw needn't show every extreme that they name: `prior_cache`: keys already rotated. `prefill_offset`: the largest value, 512, and 0 occur in every draw. `home_cache`: keys already rotated. `piece_len`: columns 0 and 2 are at most 1024 and reach it in every draw, 0 meaning no piece on that side; column 1 is 1 to 256 and reaches 256 in every draw. `side_store`: keys already rotated.
All inputs are finite; a program needn't handle non-finite values.
Results may differ from a plain program's by a relative error of at most 0.019.
The roundings to bfloat16 on the way count: a program that leaves them out, or rounds other values in their place, can miss the bound.
Values may be sent and summed in bfloat16 or wider, within the bound.
No kernel may reach another device: no remote copies, remote signals or barrier semaphores. Data moves between devices by JAX's collectives and lax.ppermute only.
A program may use at most 128 MiB of HBM per device.

v0:
```python
from functools import reduce
import math
import jax
import jax.numpy as jnp
from jax import lax
from jax.sharding import PartitionSpec as P

HD = 128
ROT = 32
EPS = 1e-05
NEG = -1e30


def with_halo(block, sides, width):
    for axis, dim in sides:
        count = lax.axis_size(axis)
        forward = [(i, i + 1) for i in range(count - 1)]
        forward.append((count - 1, 0))
        backward = [(target, source) for source, target in forward]
        low = lax.ppermute(
            lax.slice_in_dim(block, block.shape[dim] - width, None, axis=dim), axis, forward
        )
        high = lax.ppermute(lax.slice_in_dim(block, 0, width, axis=dim), axis, backward)
        block = jnp.concatenate([low, block, high], axis=dim)
    return block


def layer_norm(rows, gain, shift):
    rows = rows.astype(jnp.float32)
    middle = jnp.mean(rows, axis=-1, keepdims=True)
    centred = rows - middle
    spread = jnp.mean(centred * centred, axis=-1, keepdims=True)
    return (centred * lax.rsqrt(spread + EPS) * gain + shift).astype(jnp.bfloat16)


def rotate(vectors, positions):
    half = ROT // 2
    steps = jnp.arange(half, dtype=jnp.float32) * (2.0 / ROT)
    frequency = jnp.exp(-math.log(10000.0) * steps)
    angle = positions.astype(jnp.float32)[:, None] * frequency[None, :]
    cosine = jnp.cos(angle)[:, None, :]
    sine = jnp.sin(angle)[:, None, :]
    first = vectors[..., :half]
    second = vectors[..., half:ROT]
    return jnp.concatenate(
        [first * cosine - second * sine, second * cosine + first * sine, vectors[..., ROT:]],
        axis=-1,
    )


def project(normed, weight, bias, positions):
    count = normed.shape[0]
    width = weight.shape[2]
    mixed = jnp.dot(
        normed, weight.reshape(weight.shape[0], 3 * width), preferred_element_type=jnp.float32
    )
    mixed = (mixed + bias.reshape(1, 3 * width)).reshape(count, 3, width // HD, HD)
    query = rotate(mixed[:, 0], positions).astype(jnp.bfloat16)
    fresh_key = rotate(mixed[:, 1], positions).astype(jnp.bfloat16)
    fresh_value = mixed[:, 2].astype(jnp.bfloat16)
    return (query, fresh_key, fresh_value)


def attend_rows(query, keys, values, live):
    scores = jnp.einsum("qhd,khd->hqk", query, keys, preferred_element_type=jnp.float32) * (
        1.0 / math.sqrt(HD)
    )
    masked = jnp.where(live[None], scores, NEG)
    highest = jnp.max(masked, axis=2, keepdims=True)
    weights = jnp.where(live[None], jnp.exp(masked - highest), 0.0)
    total = jnp.sum(weights, axis=2)
    mixed = jnp.einsum(
        "hqk,khd->qhd", weights.astype(jnp.bfloat16), values, preferred_element_type=jnp.float32
    )
    return (mixed / jnp.transpose(total)[:, :, None]).astype(jnp.bfloat16)


def prefill_attend(query, fresh_key, fresh_value, prior, offset):
    count, heads = (query.shape[0], query.shape[1])
    capacity = prior.shape[1]
    keys = jnp.concatenate([prior[0].reshape(capacity, heads, HD), fresh_key], axis=0)
    values = jnp.concatenate([prior[1].reshape(capacity, heads, HD), fresh_value], axis=0)
    block = min(count, 512)

    def one_block(start):
        places = start + jnp.arange(block, dtype=jnp.int32)
        live = jnp.concatenate(
            [
                jnp.broadcast_to(jnp.arange(capacity)[None, :] < offset, (block, capacity)),
                jnp.arange(count)[None, :] <= places[:, None],
            ],
            axis=1,
        )
        return attend_rows(query, keys, values, live)

    starts = jnp.arange(count // block, dtype=jnp.int32) * block
    return lax.map(one_block, starts).reshape(count, heads * HD)


def piece_rows(query, keys, values, live):
    count, heads = (query.shape[0], query.shape[1])
    own = jnp.arange(heads)[:, None] == jnp.arange(heads)[None, :]
    spread = jnp.where(own[None, :, None, :], query[:, :, :, None], jnp.zeros((), query.dtype))
    spread = spread.reshape(count, heads * HD, heads)
    scores = jnp.einsum("rkf,rfh->rhk", keys, spread, preferred_element_type=jnp.float32) * (
        1.0 / math.sqrt(HD)
    )
    masked = jnp.where(live[:, None, :], scores, NEG)
    highest = jnp.max(masked, axis=2)
    weights = jnp.where(live[:, None, :], jnp.exp(masked - highest[:, :, None]), 0.0)
    total = jnp.sum(weights, axis=2)
    mixed = jnp.einsum(
        "rhk,rkf->rhf", weights.astype(jnp.bfloat16), values, preferred_element_type=jnp.float32
    ).reshape(count, heads, heads, HD)
    summed = jnp.sum(jnp.where(own[None, :, :, None], mixed, 0.0), axis=2)
    return (highest, total, summed)


def piece_batch(query, store, lengths):
    capacity = store.shape[2]
    live = jnp.arange(capacity)[None, :] < lengths[:, None]
    return piece_rows(query, store[:, 0], store[:, 1], live)


def home_partial(query, fresh_key, fresh_value, cache, lengths):
    count, capacity = (cache.shape[0], cache.shape[2])
    keys = jnp.concatenate([cache[:, 0], fresh_key.reshape(count, 1, -1)], axis=1)
    values = jnp.concatenate([cache[:, 1], fresh_value.reshape(count, 1, -1)], axis=1)
    live = jnp.concatenate(
        [jnp.arange(capacity)[None, :] < lengths[:, None], jnp.ones((count, 1), jnp.bool_)], axis=1
    )
    return piece_rows(query, keys, values, live)


def combine(parts):
    highest = reduce(jnp.maximum, [part[0] for part in parts])
    factors = [jnp.exp(part[0] - highest) for part in parts]
    upper = reduce(jnp.add, [factor[:, :, None] * part[2] for factor, part in zip(factors, parts)])
    lower = reduce(jnp.add, [factor * part[1] for factor, part in zip(factors, parts)])
    return (upper / lower[:, :, None]).astype(jnp.bfloat16)


def local(
    prefill_x,
    decode_x,
    ln_gain,
    ln_bias,
    qkv_weight,
    qkv_bias,
    prior_cache,
    prefill_offset,
    home_cache,
    piece_len,
    side_store,
):
    count = prefill_x.shape[0]
    requests = decode_x.shape[0]
    rows = jnp.concatenate([prefill_x, decode_x], axis=0)
    partner = lax.ppermute(rows, "tz", [(0, 1), (1, 0)])
    own_y = lax.all_gather(rows, "ty", axis=1, tiled=True)
    partner_y = lax.all_gather(partner, "ty", axis=1, tiled=True)
    whole = jnp.concatenate([own_y, partner_y], axis=1)
    z = lax.axis_index("tz")

    def feature_order(table):
        blocks = table.reshape((-1, 2, rows.shape[1]) + table.shape[1:])
        own = lax.dynamic_index_in_dim(blocks, z, 1, keepdims=False)
        other = lax.dynamic_index_in_dim(blocks, 1 - z, 1, keepdims=False)
        return jnp.concatenate([own, other], axis=0).reshape(table.shape)

    normed = layer_norm(whole, feature_order(ln_gain), feature_order(ln_bias))
    qkv_weight = feature_order(qkv_weight)
    positions = jnp.concatenate(
        [
            prefill_offset[0] + jnp.arange(count, dtype=jnp.int32),
            piece_len[:, 0] + piece_len[:, 1] + piece_len[:, 2],
        ],
        axis=0,
    )
    query, fresh_key, fresh_value = project(normed, qkv_weight, qkv_bias, positions)
    own_query = query[count:]
    home_parts = home_partial(
        own_query, fresh_key[count:], fresh_value[count:], home_cache, piece_len[:, 1]
    )
    groups = lax.axis_size("group")
    forward = [(i, (i + 1) % groups) for i in range(groups)]
    backward = [((i + 1) % groups, i) for i in range(groups)]
    heads = own_query.shape[1]

    def ask(lengths, pairs):
        packed = jnp.concatenate(
            [
                own_query.astype(jnp.float32).reshape(requests, -1),
                lengths[:, None].astype(jnp.float32),
            ],
            axis=1,
        )
        got = lax.ppermute(packed, "group", pairs)
        return (
            got[:, :-1].reshape(own_query.shape).astype(own_query.dtype),
            got[:, -1].astype(jnp.int32),
        )

    def answer(parts, pairs):
        highest, total, summed = parts
        packed = jnp.concatenate([summed, highest[:, :, None], total[:, :, None]], axis=2)
        got = lax.ppermute(packed, "group", pairs)
        return (got[:, :, HD], got[:, :, HD + 1], got[:, :, :HD])

    prev_query, prev_len = ask(piece_len[:, 2], forward)
    next_query, next_len = ask(piece_len[:, 0], backward)
    right_parts = answer(piece_batch(prev_query, side_store[:requests], prev_len), backward)
    left_parts = answer(piece_batch(next_query, side_store[requests:], next_len), forward)
    prefill_out = prefill_attend(
        query[:count], fresh_key[:count], fresh_value[:count], prior_cache[0], prefill_offset[0]
    )
    decode_out = combine([left_parts, home_parts, right_parts]).reshape(requests, -1)
    return (prefill_out, decode_out)


def solution(mesh):
    devices = mesh.devices.reshape(mesh.devices.shape[0], -1, 2)
    split = jax.sharding.Mesh(devices, ("group", "ty", "tz"))
    tp = ("ty", "tz")
    inner = jax.shard_map(
        local,
        mesh=split,
        in_specs=(
            P("group", tp),
            P("group", tp),
            P(),
            P(),
            P(None, None, tp),
            P(None, tp),
            P("group", None, None, tp),
            P("group"),
            P("group", None, None, tp),
            P("group", None),
            P("group", None, None, tp),
        ),
        out_specs=(P("group", tp), P("group", tp)),
        check_vma=False,
    )
    return inner
```

profile of v0, /device:TPU:8, one launch (start us, length us, event | category | flops | bytes accessed | tf_op | source)
XLA Modules:
  0.0 141.7 jit_solution(1339242411152558257)
XLA Ops:
  7.2 1.1 constant_dynamic-update-slice_fusion.1
  9.0 0.8 copy-done.2
  9.9 7.3 %collective-permute-start = (bf16[516,512]{1,0:T(8,128)(2,1)}, bf16[516,512]{1,0:T(8,128)(2,1)S(1)}, u32[]{:S(2)}, u32[]{:S(2)}) collective-permute-start(bf16[516,512]{1,0:T(8,128)(2,1)} %copy-done.2), channel_id=1, source_target_pairs={{0,1},{1,0},{2,3},{3,2},{4,5},{5,4},{6,7},{7,6},{8,9},{9,8},{10,11... | collective-permute-start | bytes 1585160 | tf_op jit(solution)/shard_map/ppermute | solution.py:159
  17.1 14.6 %collective-permute-done = bf16[516,512]{1,0:T(8,128)(2,1)S(1)} collective-permute-done((bf16[516,512]{1,0:T(8,128)(2,1)}, bf16[516,512]{1,0:T(8,128)(2,1)S(1)}, u32[]{:S(2)}, u32[]{:S(2)}) %collective-permute-start) | collective-permute-done | bytes 528416 | tf_op jit(solution)/shard_map/ppermute | solution.py:159
  31.7 0.8 copy-done.4
  32.5 6.3 %constant_dynamic-slice_fusion.1 = (bf16[4,1,512,3,256]{4,2,1,0,3:T(8,128)(2,1)}, bf16[4,1,512,3,256]{4,2,1,0,3:T(8,128)(2,1)}) fusion(bf16[4,2,512,3,256]{4,2,1,0,3:T(8,128)(2,1)} %bitcast.138, s32[]{:T(128)S(6)} %select_n.64, s32[]{:T(128)S(6)} %select_n.65), kind=kLoop, calls=%fused_computation.135 | loop fusion | bytes 12582920 | tf_op jit(solution)/shard_map/jit(dynamic_index_in_dim)/dynamic_slice | solution.py:167
  38.8 4.8 %copy.162 = bf16[4,1,512,3,256]{2,0,4,3,1:T(4,128)(2,1)S(1)} copy(bf16[4,1,512,3,256]{4,2,1,0,3:T(8,128)(2,1)} %get-tuple-element.42) | data formatting | bytes 6291456 | tf_op jit(solution)/shard_map/jit(dynamic_index_in_dim)/dynamic_slice | solution.py:168
  43.6 6.2 %copy.161 = bf16[4,1,512,3,256]{2,0,4,3,1:T(4,128)(2,1)} copy(bf16[4,1,512,3,256]{4,2,1,0,3:T(8,128)(2,1)} %get-tuple-element.41) | data formatting | bytes 6291456 | tf_op jit(solution)/shard_map/jit(dynamic_index_in_dim)/dynamic_slice | solution.py:167
  49.8 4.5 %pad_maximum_fusion = bf16[8,512,3,256]{1,0,3,2:T(8,128)(2,1)S(1)} fusion(bf16[4,512,3,256]{1,0,3,2:T(4,128)(2,1)S(1)} %bitcast.132, bf16[4,512,3,256]{1,0,3,2:T(4,128)(2,1)} %bitcast.133), kind=kLoop, calls=%fused_computation.9 | loop fusion | flops 12582912 | bytes 12582912 | tf_op jit(solution)/shard_map/concatenate | solution.py:169
  54.4 6.8 %copy.215 = bf16[96,8,8,512]{3,1,2,0:T(8,128)(2,1)} copy(bf16[96,8,8,512]{3,2,1,0:T(8,128)(2,1)S(1)} %bitcast.131) | data formatting | bytes 12582912
  63.5 0.8 copy.160
  64.7 1.0 pad_add_fusion
  65.7 1.1 slice_bitcast_fusion.1
  66.8 14.4 %all-gather.5.cloned.1.call-done = bf16[516,2048]{1,0:T(8,128)(2,1)} async-done(((bf16[516,512]{1,0:T(8,128)(2,1)}), bf16[516,2048]{1,0:T(8,128)(2,1)}) %all-gather.5.cloned.1.call-update) | async-done | bytes 2113552 | tf_op jit(solution)/shard_map/all_gather | solution.py:161
  81.1 3.0 %convert_reduce_fusion = f32[516]{0:T(1024)S(1)} fusion(bf16[516,2048]{1,0:T(8,128)(2,1)} %all-gather.5.cloned.1.call-done, bf16[516,2048]{1,0:T(8,128)(2,1)} %all-gather.3.cloned.1.call-done), kind=kLoop, calls=%fused_computation.2 | loop fusion | flops 10567164 | bytes 4229136 | tf_op jit(solution)/shard_map/reduce_sum | solution.py:30
  84.2 3.0 %fusion.3 = f32[516]{0:T(1024)S(1)} fusion(f32[516]{0:T(1024)S(1)} %broadcast_multiply_fusion, bf16[516,2048]{1,0:T(8,128)(2,1)S(1)} %copy-done.1, bf16[516,2048]{1,0:T(8,128)(2,1)S(1)} %copy-done), kind=kLoop, calls=%fused_computation.5 | loop fusion | flops 14794236 | bytes 4231200 | tf_op jit(solution)/shard_map/reduce_sum | solution.py:32
  87.3 8.0 %fusion.31 = f32[516,768]{1,0:T(8,128)} fusion(bf16[4096,768]{0,1:T(8,128)(2,1)} %bitcast.139, f32[4096]{0:T(1024)S(1)} %bitcast.148, f32[4096]{0:T(1024)S(1)} %bitcast.149, f32[516]{0:T(1024)S(1)} %add_rsqrt_fusion, f32[516]{0:T(1024)S(1)} %broadcast_multiply_fusion, bf16[516,2048]{1,0:T(8,128)(2,1)S(1)} %copy-done.1, bf16[516,2048]{1,0:T(8,128)(2,1)S(1)} %copy-done, ...), kind=kOutput, calls=%fused_computation.37 | convolution fusion | flops 3265809408 | bytes 12143648 | tf_op jit(solution)/shard_map/dot_general | solution.py:54
  95.3 2.1 %reshape.239 = f32[516,3,2,128]{3,2,1,0:T(2,128)S(1)} reshape(f32[516,768]{1,0:T(8,128)} %fusion.31) | data formatting | bytes 3170304 | tf_op jit(solution)/shard_map/reshape | solution.py:57
  97.8 2.2 %copy.163 = bf16[516,3,2,128]{0,3,2,1:T(8,128)(2,1)} copy(f32[516,3,2,128]{3,2,1,0:T(2,128)S(1)} %reshape.239) | data formatting | bytes 2377728 | tf_op jit(solution)/shard_map/reshape | solution.py:57
  101.1 1.0 slice_bitcast_fusion.2
  102.1 0.8 slice.182
  103.5 5.6 %collective-permute-start.1 = (f32[4,257]{1,0:T(4,128)S(1)}, f32[4,257]{1,0:T(4,128)S(1)}, u32[]{:S(2)}, u32[]{:S(2)}) collective-permute-start(f32[4,257]{1,0:T(4,128)S(1)} %get-tuple-element.63), channel_id=1, source_target_pairs={{8,0},{16,8},{24,16},{32,24},{40,32},{48,40},{56,48},{64,56},{72,6... | collective-permute-start | bytes 12344 | tf_op jit(solution)/shard_map/ppermute | solution.py:198
  109.2 0.7 fusion.66
  110.0 2.4 %fusion.110 = (f32[2,512]{1,0:T(2,128)S(1)}, bf16[2,512,1024]{2,1,0:T(8,128)(2,1)S(1)}) fusion(f32[2,512,1024]{2,1,0:T(8,128)S(1)} %fusion.66, pred[512,1024]{1,0:T(8,128)(4,1)S(1)} %copy-done.5), kind=kOutput, calls=%fused_computation.173 | output fusion | flops 8389631 | bytes 6819840 | tf_op jit(solution)/shard_map/while/body/eval_jaxpr/sub | solution.py:70
  112.3 0.8 fusion.40
  114.2 2.3 %fusion.111 = (f32[4,2]{1,0:T(4,128)S(1)}, f32[4,2,1024]{2,1,0:T(2,128)S(1)}) fusion(bf16[8,2,1024,256]{3,2,1,0:T(8,128)(2,1)} %param.21, pred[256,2]{0,1:T(4,128)(4,1)S(1)} %bitcast.156, bf16[4,256]{1,0:T(4,128)(2,1)S(1)} %slice.263, pred[4,1024]{1,0:T(4,128)(4,1)S(1)} %iota_compare_fusion.1), kind=kOutput, calls=%fused_computation.174 | convolution fusion | flops 4220920 | bytes 2136608 | tf_op jit(solution)/shard_map/rkf,rfh->rhk/dot_general | solution.py:105
  116.5 2.0 %fusion.14 = f32[4,2,256]{2,1,0:T(2,128)S(1)} fusion(bf16[8,2,1024,256]{3,2,1,0:T(8,128)(2,1)} %param.21, f32[4,2,1024]{2,1,0:T(2,128)S(1)} %get-tuple-element.73, pred[4,1024]{1,0:T(4,128)(4,1)S(1)} %iota_compare_fusion.1, f32[4,2]{1,0:T(4,128)S(1)} %get-tuple-element.72), kind=kOutput, calls=%fused_computation.19 | convolution fusion | flops 4218880 | bytes 2142240 | tf_op jit(solution)/shard_map/rhk,rkf->rhf/dot_general | solution.py:112
  119.0 2.3 %fusion.112 = (f32[4,2]{1,0:T(4,128)S(1)}, f32[4,2,1024]{2,1,0:T(2,128)S(1)}) fusion(bf16[8,2,1024,256]{3,2,1,0:T(8,128)(2,1)} %param.21, pred[256,2]{0,1:T(4,128)(4,1)S(1)} %bitcast.157, bf16[4,256]{1,0:T(4,128)(2,1)S(1)} %slice.264, pred[4,1024]{1,0:T(4,128)(4,1)S(1)} %iota_compare_fusion.2), kind=kOutput, calls=%fused_computation.175 | convolution fusion | flops 4220920 | bytes 2136608 | tf_op jit(solution)/shard_map/rkf,rfh->rhk/dot_general | solution.py:105
  121.4 2.0 %fusion.18 = f32[4,2,256]{2,1,0:T(2,128)S(1)} fusion(bf16[8,2,1024,256]{3,2,1,0:T(8,128)(2,1)} %param.21, f32[4,2,1024]{2,1,0:T(2,128)S(1)} %get-tuple-element.75, pred[4,1024]{1,0:T(4,128)(4,1)S(1)} %iota_compare_fusion.2, f32[4,2]{1,0:T(4,128)S(1)} %get-tuple-element.74), kind=kOutput, calls=%fused_computation.23 | convolution fusion | flops 4218880 | bytes 2142240 | tf_op jit(solution)/shard_map/rhk,rkf->rhf/dot_general | solution.py:112
  125.4 0.8 copy.195
  126.3 2.1 %collective-permute-done.4 = f32[4,2,130]{0,1,2:T(2,128)S(1)} collective-permute-done((f32[4,2,130]{0,1,2:T(2,128)S(1)}, f32[4,2,130]{0,1,2:T(2,128)S(1)}, u32[]{:S(2)}, u32[]{:S(2)}) %collective-permute-start.4) | collective-permute-done | bytes 4192 | tf_op jit(solution)/shard_map/ppermute | solution.py:207
  128.5 4.9 %collective-permute-done.2 = f32[4,2,130]{0,1,2:T(2,128)S(1)} collective-permute-done((f32[4,2,130]{0,1,2:T(2,128)S(1)}, f32[4,2,130]{0,1,2:T(2,128)S(1)}, u32[]{:S(2)}, u32[]{:S(2)}) %collective-permute-start.2) | collective-permute-done | bytes 4192 | tf_op jit(solution)/shard_map/ppermute | solution.py:207
  (122 shorter events, 9.5 us)
Async XLA Ops:
  7.2 59.6 %all-gather.3.cloned.1.call-start = ((), (), s32[]{:S(2)}) async-start(), calls=%async_computation | async-start | bytes 2662400 | tf_op jit(solution)/shard_map/all_gather | solution.py:160
  9.0 0.8 copy-start.2
  9.8 71.3 %all-gather.5.cloned.1.call-start = ((), (), s32[]{:S(2)}) async-start(), calls=%async_computation.1 | async-start | bytes 2662400 | tf_op jit(solution)/shard_map/all_gather | solution.py:161
  9.9 21.8 %collective-permute-start = (bf16[516,512]{1,0:T(8,128)(2,1)}, bf16[516,512]{1,0:T(8,128)(2,1)S(1)}, u32[]{:S(2)}, u32[]{:S(2)}) collective-permute-start(bf16[516,512]{1,0:T(8,128)(2,1)} %copy-done.2), channel_id=1, source_target_pairs={{0,1},{1,0},{2,3},{3,2},{4,5},{5,4},{6,7},{7,6},{8,9},{9,8},{10,11... | collective-permute-start | bytes 1585160 | tf_op jit(solution)/shard_map/ppermute | solution.py:159
  31.7 0.8 copy-start.4
  54.3 6.9 %copy-start.11 = (f32[4096]{0:T(1024)S(1)}, f32[4096]{0:T(1024)}, u32[]{:S(2)}) copy-start(f32[4096]{0:T(1024)} %param.14) | copy-start | bytes 49156
  54.3 6.9 %copy-start.12 = (f32[4096]{0:T(1024)S(1)}, f32[4096]{0:T(1024)}, u32[]{:S(2)}) copy-start(f32[4096]{0:T(1024)} %param.13) | copy-start | bytes 49156
  54.3 7.1 %copy-start.13 = (f32[3,256]{1,0:T(4,128)S(1)}, f32[3,256]{1,0:T(4,128)}, u32[]{:S(2)}) copy-start(f32[3,256]{1,0:T(4,128)} %param.16) | copy-start | bytes 9220
  54.4 8.0 %copy-start.10 = (s32[4,3]{1,0:T(4,128)S(1)}, s32[4,3]{1,0:T(4,128)}, u32[]{:S(2)}) copy-start(s32[4,3]{1,0:T(4,128)} %param.20) | copy-start | bytes 148
  54.4 8.7 %copy-start.6 = (bf16[1,2,512,256]{3,2,1,0:T(8,128)(2,1)S(1)}, bf16[1,2,512,256]{3,2,1,0:T(8,128)(2,1)}, u32[]{:S(2)}) copy-start(bf16[1,2,512,256]{3,2,1,0:T(8,128)(2,1)} %param.17) | copy-start | bytes 1572868
  61.2 4.4 %copy-start.3 = (bf16[4,2,256,256]{3,2,1,0:T(8,128)(2,1)S(1)}, bf16[4,2,256,256]{3,2,1,0:T(8,128)(2,1)}, u32[]{:S(2)}) copy-start(bf16[4,2,256,256]{3,2,1,0:T(8,128)(2,1)} %param.19) | copy-start | bytes 3145732
  66.8 17.4 %copy-start = (bf16[516,2048]{1,0:T(8,128)(2,1)S(1)}, bf16[516,2048]{1,0:T(8,128)(2,1)}, u32[]{:S(2)}) copy-start(bf16[516,2048]{1,0:T(8,128)(2,1)} %all-gather.3.cloned.1.call-done) | copy-start | bytes 6340612
  81.1 3.1 %copy-start.1 = (bf16[516,2048]{1,0:T(8,128)(2,1)S(1)}, bf16[516,2048]{1,0:T(8,128)(2,1)}, u32[]{:S(2)}) copy-start(bf16[516,2048]{1,0:T(8,128)(2,1)} %all-gather.5.cloned.1.call-done) | copy-start | bytes 6340612
  101.1 8.8 %copy-start.5 = (pred[512,1024]{1,0:T(8,128)(4,1)S(1)}, pred[512,1024]{1,0:T(8,128)(4,1)}, u32[]{:S(2)}) copy-start(pred[512,1024]{1,0:T(8,128)(4,1)} %pad_add_fusion) | copy-start | bytes 1572868
  103.4 10.6 %collective-permute-start.3 = (f32[4,257]{1,0:T(4,128)S(1)}, f32[4,257]{1,0:T(4,128)S(1)}, u32[]{:S(2)}, u32[]{:S(2)}) collective-permute-start(f32[4,257]{1,0:T(4,128)S(1)} %get-tuple-element.64), channel_id=1, source_target_pairs={{0,8},{8,16},{16,24},{24,32},{32,40},{40,48},{48,56},{56,64},{64,7... | collective-permute-start | bytes 12344 | tf_op jit(solution)/shard_map/ppermute | solution.py:198
  103.5 15.4 %collective-permute-start.1 = (f32[4,257]{1,0:T(4,128)S(1)}, f32[4,257]{1,0:T(4,128)S(1)}, u32[]{:S(2)}, u32[]{:S(2)}) collective-permute-start(f32[4,257]{1,0:T(4,128)S(1)} %get-tuple-element.63), channel_id=1, source_target_pairs={{8,0},{16,8},{24,16},{32,24},{40,32},{48,40},{56,48},{64,56},{72,6... | collective-permute-start | bytes 12344 | tf_op jit(solution)/shard_map/ppermute | solution.py:198
  109.9 2.4 %copy-start.9 = (bf16[1,1,512,256]{2,3,1,0:T(8,128)(2,1)S(1)}, bf16[1,1,512,256]{2,3,1,0:T(8,128)(2,1)}, u32[]{:S(2)}) copy-start(bf16[1,1,512,256]{2,3,1,0:T(8,128)(2,1)} %copy.160) | copy-start | bytes 786436
  112.3 1.0 copy-start.8
  112.3 1.4 copy-start.7
  124.1 4.2 %collective-permute-start.4 = (f32[4,2,130]{0,1,2:T(2,128)S(1)}, f32[4,2,130]{0,1,2:T(2,128)S(1)}, u32[]{:S(2)}, u32[]{:S(2)}) collective-permute-start(f32[4,2,130]{0,1,2:T(2,128)S(1)} %pad_maximum_fusion.6), channel_id=1, source_target_pairs={{8,0},{16,8},{24,16},{32,24},{40,32},{48,40},{56,48},{64,56},{72,6... | collective-permute-start | bytes 12488 | tf_op jit(solution)/shard_map/ppermute | solution.py:207
  125.0 8.4 %collective-permute-start.2 = (f32[4,2,130]{0,1,2:T(2,128)S(1)}, f32[4,2,130]{0,1,2:T(2,128)S(1)}, u32[]{:S(2)}, u32[]{:S(2)}) collective-permute-start(f32[4,2,130]{0,1,2:T(2,128)S(1)} %pad_maximum_fusion.5), channel_id=1, source_target_pairs={{0,8},{8,16},{16,24},{24,32},{32,40},{40,48},{48,56},{56,64},{64,7... | collective-permute-start | bytes 12488 | tf_op jit(solution)/shard_map/ppermute | solution.py:207
Sparse Core Ops, SparseCore 0:
  9.9 35.5 all-gather.2
  47.4 33.7 all-gather.4
where the time goes:
time: 142 us
  local copies, waits for them, and re-layouts  40.7 us (29%)
  waiting for transfers between devices  35.9 us (25%)
  matrix products  18.9 us (13%)
  other arithmetic  17 us (12%)
  between operations  15.4 us (11%)
  starting transfers between devices  13.7 us (10%)
    ppermute x1, waiting for transfers between devices, local(): partner = lax.ppermute(rows, 'tz', [(0, 1), (1, 0)])  14.6 us
    all_gather x1, waiting for transfers between devices, local(): partner_y = lax.all_gather(partner, 'ty', axis=1, tiled=True)  14.4 us
    dynamic_slice x3, local copies, waits for them, and re-layouts, feature_order(): own = lax.dynamic_index_in_dim(blocks, z, 1, keepdims=False)  12.5 us
    unnamed x46, local copies, waits for them, and re-layouts  11.3 us
    dot_general x1, matrix products, project(): jnp.dot(normed, weight.reshape(weight.shape[0], 3 * width), preferred_ele...  8.04 us
    ppermute x1, starting transfers between devices, local(): partner = lax.ppermute(rows, 'tz', [(0, 1), (1, 0)])  7.28 us
    ppermute x2, waiting for transfers between devices, answer(): got = lax.ppermute(packed, 'group', pairs)  6.96 us
    ppermute x2, starting transfers between devices, ask(): got = lax.ppermute(packed, 'group', pairs)  5.72 us
  transfers between devices with their start and end apart: 7, of which 4 were waited for; matrix products, arithmetic and copies ran while one was open for 31% of the time, Pallas kernels for 0%

commit v1 on v0

--- a/solution.py
+++ b/solution.py
@@ -157,8 +157,11 @@
     requests = decode_x.shape[0]
     rows = jnp.concatenate([prefill_x, decode_x], axis=0)
     partner = lax.ppermute(rows, "tz", [(0, 1), (1, 0)])
-    own_y = lax.all_gather(rows, "ty", axis=1, tiled=True)
-    partner_y = lax.all_gather(partner, "ty", axis=1, tiled=True)
+    own_y, partner_y = jnp.split(
+        lax.all_gather(jnp.concatenate([rows, partner], axis=0), "ty", axis=1, tiled=True),
+        [rows.shape[0]],
+        axis=0,
+    )
     whole = jnp.concatenate([own_y, partner_y], axis=1)
     z = lax.axis_index("tz")
 

time: 142 us -> 154 us (1.085)
  waiting for transfers between devices: 35.9 us -> 42 us
  local copies, waits for them, and re-layouts: 40.7 us -> 46.2 us
  starting transfers between devices: 13.7 us -> 18.6 us
  matrix products: 18.9 us -> 15 us
    all_gather x2 -> x1, waiting for transfers between devices: 14.4 us -> 26.2 us  [local(): lax.all_gather(jnp.concatenate([rows, partner], axis=0), 'ty', axis=1, ti...]
    concatenate x1, local copies, waits for them, and re-layouts: 0.7 us -> 7.36 us  [local(): jnp.concatenate([rows, partner], axis=0)]
    ppermute x2, waiting for transfers between devices: 6.96 us -> 1.4 us  [answer(): got = lax.ppermute(packed, 'group', pairs)]
    ppermute x2, starting transfers between devices: 0.66 us -> 5.8 us  [answer(): got = lax.ppermute(packed, 'group', pairs)]
    dot_general x1, matrix products: 8.04 us -> 4.18 us  [project(): jnp.dot(normed, weight.reshape(weight.shape[0], 3 * width), preferred_ele...]
    split x0 -> x1, local copies, waits for them, and re-layouts: none -> 3.09 us  [local(): jnp.split(lax.all_gather(jnp.concatenate([rows, partner], axis=0), 'ty',...]
    unnamed x46 -> x45, local copies, waits for them, and re-layouts: 11.3 us -> 8.63 us
    reduce_sum x1, other arithmetic: 3.03 us -> 0.64 us  [layer_norm(): middle = jnp.mean(rows, axis=-1, keepdims=True)]
  transfers between devices with their start and end apart: 7 -> 6, of which waited for: 4 -> 3; matrix products, arithmetic and copies ran while one was open for 31% -> 29% of each run, Pallas kernels for 0% -> 0%
where the time goes in v1:
time: 154 us; the launch traced here: 153 us
  local copies, waits for them, and re-layouts  46.2 us (30%)
  waiting for transfers between devices  42 us (27%)
  starting transfers between devices  18.6 us (12%)
  other arithmetic  16.3 us (11%)
  between operations  15.3 us (10%)
  matrix products  15 us (10%)
    all_gather x1, waiting for transfers between devices, local(): lax.all_gather(jnp.concatenate([rows, partner], axis=0), 'ty', axis=1, ti...  26.2 us
    ppermute x1, waiting for transfers between devices, local(): partner = lax.ppermute(rows, 'tz', [(0, 1), (1, 0)])  14.4 us
    dynamic_slice x3, local copies, waits for them, and re-layouts, feature_order(): own = lax.dynamic_index_in_dim(blocks, z, 1, keepdims=False)  11.3 us
    unnamed x45, local copies, waits for them, and re-layouts  8.63 us
    concatenate x1, local copies, waits for them, and re-layouts, local(): jnp.concatenate([rows, partner], axis=0)  7.36 us
    ppermute x1, starting transfers between devices, local(): partner = lax.ppermute(rows, 'tz', [(0, 1), (1, 0)])  7.28 us
    ppermute x2, starting transfers between devices, answer(): got = lax.ppermute(packed, 'group', pairs)  5.8 us
    ppermute x2, starting transfers between devices, ask(): got = lax.ppermute(packed, 'group', pairs)  5.45 us
  transfers between devices with their start and end apart: 6, of which 3 were waited for; matrix products, arithmetic and copies ran while one was open for 29% of the time, Pallas kernels for 0%

profile of v1, /device:TPU:8, one launch (start us, length us, event | category | flops | bytes accessed | tf_op | source)
XLA Modules:
  0.0 153.4 jit_solution(15414271596243162566)
XLA Ops:
  7.2 1.1 pad_maximum_fusion.3
  8.3 7.3 %collective-permute-start = (bf16[516,512]{1,0:T(8,128)(2,1)S(1)}, bf16[516,512]{1,0:T(8,128)(2,1)S(1)}, u32[]{:S(2)}, u32[]{:S(2)}) collective-permute-start(bf16[516,512]{1,0:T(8,128)(2,1)S(1)} %pad_maximum_fusion.3), channel_id=1, source_target_pairs={{0,1},{1,0},{2,3},{3,2},{4,5},{5,4},{6,7},{7,6},{8,9},{9,8},{10,11... | collective-permute-start | bytes 1585160 | tf_op jit(solution)/shard_map/ppermute | solution.py:159
  15.6 14.4 %collective-permute-done = bf16[516,512]{1,0:T(8,128)(2,1)S(1)} collective-permute-done((bf16[516,512]{1,0:T(8,128)(2,1)S(1)}, bf16[516,512]{1,0:T(8,128)(2,1)S(1)}, u32[]{:S(2)}, u32[]{:S(2)}) %collective-permute-start) | collective-permute-done | bytes 528416 | tf_op jit(solution)/shard_map/ppermute | solution.py:159
  30.0 7.4 %concatenate.68 = bf16[1032,512]{1,0:T(8,128)(2,1)} concatenate(bf16[512,512]{1,0:T(8,128)(2,1)} %param.11, bf16[4,512]{1,0:T(4,128)(2,1)} %param.12, bf16[516,512]{1,0:T(8,128)(2,1)S(1)} %collective-permute-done), dimensions={0} | concatenate | bytes 2113536 | tf_op jit(solution)/shard_map/concatenate | solution.py:161
  37.6 5.1 %constant_dynamic-slice_fusion.1 = (bf16[4,1,512,3,256]{4,2,1,0,3:T(8,128)(2,1)}, bf16[4,1,512,3,256]{4,2,1,0,3:T(8,128)(2,1)S(1)}) fusion(bf16[4,2,512,3,256]{4,2,1,0,3:T(8,128)(2,1)} %bitcast.138, s32[]{:T(128)S(6)} %select_n.64, s32[]{:T(128)S(6)} %select_n.65), kind=kLoop, calls=%fused_computation.134 | loop fusion | bytes 12582920 | tf_op jit(solution)/shard_map/jit(dynamic_index_in_dim)/dynamic_slice | solution.py:170
  42.6 6.2 %copy.161 = bf16[4,1,512,3,256]{2,0,4,3,1:T(4,128)(2,1)} copy(bf16[4,1,512,3,256]{4,2,1,0,3:T(8,128)(2,1)} %get-tuple-element.41) | data formatting | bytes 6291456 | tf_op jit(solution)/shard_map/jit(dynamic_index_in_dim)/dynamic_slice | solution.py:170
  48.8 4.4 %copy.162 = bf16[4,1,512,3,256]{2,0,4,3,1:T(4,128)(2,1)} copy(bf16[4,1,512,3,256]{4,2,1,0,3:T(8,128)(2,1)S(1)} %get-tuple-element.42) | data formatting | bytes 6291456 | tf_op jit(solution)/shard_map/jit(dynamic_index_in_dim)/dynamic_slice | solution.py:171
  53.2 5.1 %pad_maximum_fusion = bf16[8,512,3,256]{1,0,3,2:T(8,128)(2,1)S(1)} fusion(bf16[4,512,3,256]{1,0,3,2:T(4,128)(2,1)} %bitcast.133, bf16[4,512,3,256]{1,0,3,2:T(4,128)(2,1)} %bitcast.132), kind=kLoop, calls=%fused_computation.9 | loop fusion | flops 12582912 | bytes 12582912 | tf_op jit(solution)/shard_map/concatenate | solution.py:172
  58.4 6.8 %copy.215 = bf16[96,8,8,512]{3,1,2,0:T(8,128)(2,1)} copy(bf16[96,8,8,512]{3,2,1,0:T(8,128)(2,1)S(1)} %bitcast.131) | data formatting | bytes 12582912
  66.6 0.9 copy.166
  67.9 0.8 copy.169
  68.7 0.9 copy.160
  69.8 1.0 pad_add_fusion
  70.8 1.0 slice_bitcast_fusion.1
  71.8 26.2 %all-gather.2.cloned.1.call-done = bf16[1032,2048]{1,0:T(8,128)(2,1)} async-done(((bf16[1032,512]{1,0:T(8,128)(2,1)}), bf16[1032,2048]{1,0:T(8,128)(2,1)}) %all-gather.2.cloned.1.call-update) | async-done | bytes 4227088 | tf_op jit(solution)/shard_map/all_gather | solution.py:161
  98.0 3.1 %fusion.108 = (bf16[516,2048]{1,0:T(8,128)(2,1)S(1)}, bf16[516,2048]{1,0:T(8,128)(2,1)S(1)}) fusion(bf16[1032,2048]{1,0:T(8,128)(2,1)} %all-gather.2.cloned.1.call-done), kind=kLoop, calls=%fused_computation.170 | loop fusion | bytes 8454144 | tf_op jit(solution)/shard_map/split | solution.py:160
  101.8 3.0 %fusion.3 = f32[516]{0:T(1024)S(1)} fusion(f32[516]{0:T(1024)S(1)} %broadcast_multiply_fusion, bf16[516,2048]{1,0:T(8,128)(2,1)S(1)} %get-tuple-element.44, bf16[516,2048]{1,0:T(8,128)(2,1)S(1)} %get-tuple-element.43), kind=kLoop, calls=%fused_computation.5 | loop fusion | flops 14794236 | bytes 4231200 | tf_op jit(solution)/shard_map/reduce_sum | solution.py:32
  104.9 4.2 %fusion.31 = f32[516,768]{1,0:T(8,128)S(1)} fusion(bf16[4096,768]{0,1:T(8,128)(2,1)S(1)} %bitcast.141, f32[4096]{0:T(1024)S(1)} %bitcast.151, f32[4096]{0:T(1024)S(1)} %bitcast.150, f32[516]{0:T(1024)S(1)} %add_rsqrt_fusion, f32[516]{0:T(1024)S(1)} %broadcast_multiply_fusion, bf16[516,2048]{1,0:T(8,128)(2,1)S(1)} %get-tuple-element.44, ...), kind=kOutput, calls=%fused_computation.37 | convolution fusion | flops 3265809408 | bytes 12143648 | tf_op jit(solution)/shard_map/dot_general | solution.py:54
  109.1 0.8 reshape.239
  110.3 2.2 %copy.163 = bf16[516,3,2,128]{0,3,2,1:T(8,128)(2,1)} copy(f32[516,3,2,128]{3,2,1,0:T(2,128)S(1)} %reshape.239) | data formatting | bytes 2377728 | tf_op jit(solution)/shard_map/reshape | solution.py:57
  114.0 0.8 slice.182
  114.8 1.0 slice_bitcast_fusion.2
  115.8 5.2 %collective-permute-start.1 = (f32[4,257]{1,0:T(4,128)S(1)}, f32[4,257]{1,0:T(4,128)S(1)}, u32[]{:S(2)}, u32[]{:S(2)}) collective-permute-start(f32[4,257]{1,0:T(4,128)S(1)} %get-tuple-element.65), channel_id=1, source_target_pairs={{8,0},{16,8},{24,16},{32,24},{40,32},{48,40},{56,48},{64,56},{72,6... | collective-permute-start | bytes 12344 | tf_op jit(solution)/shard_map/ppermute | solution.py:201
  122.1 2.3 %fusion.111 = (f32[2,512]{1,0:T(2,128)S(1)}, bf16[2,512,1024]{2,1,0:T(8,128)(2,1)S(1)}) fusion(f32[2,512,1024]{2,1,0:T(8,128)S(1)} %fusion.66, pred[512,1024]{1,0:T(8,128)(4,1)S(1)} %copy-done.3), kind=kOutput, calls=%fused_computation.173 | output fusion | flops 8389631 | bytes 6819840 | tf_op jit(solution)/shard_map/while/body/eval_jaxpr/sub | solution.py:70
  124.5 0.8 fusion.40
  126.3 2.3 %fusion.113 = (f32[4,2]{1,0:T(4,128)S(1)}, f32[4,2,1024]{2,1,0:T(2,128)S(1)}) fusion(bf16[8,2,1024,256]{3,2,1,0:T(8,128)(2,1)} %param.21, pred[256,2]{0,1:T(4,128)(4,1)S(1)} %bitcast.158, bf16[4,256]{1,0:T(4,128)(2,1)S(1)} %slice.264, pred[4,1024]{1,0:T(4,128)(4,1)S(1)} %iota_compare_fusion.2), kind=kOutput, calls=%fused_computation.175 | convolution fusion | flops 4220920 | bytes 2136608 | tf_op jit(solution)/shard_map/rkf,rfh->rhk/dot_general | solution.py:105
  128.7 2.0 %fusion.18 = f32[4,2,256]{2,1,0:T(2,128)S(1)} fusion(bf16[8,2,1024,256]{3,2,1,0:T(8,128)(2,1)} %param.21, f32[4,2,1024]{2,1,0:T(2,128)S(1)} %get-tuple-element.77, pred[4,1024]{1,0:T(4,128)(4,1)S(1)} %iota_compare_fusion.2, f32[4,2]{1,0:T(4,128)S(1)} %get-tuple-element.76), kind=kOutput, calls=%fused_computation.23 | convolution fusion | flops 4218880 | bytes 2142240 | tf_op jit(solution)/shard_map/rhk,rkf->rhf/dot_general | solution.py:112
  131.2 2.3 %fusion.112 = (f32[4,2]{1,0:T(4,128)S(1)}, f32[4,2,1024]{2,1,0:T(2,128)S(1)}) fusion(bf16[8,2,1024,256]{3,2,1,0:T(8,128)(2,1)} %param.21, pred[256,2]{0,1:T(4,128)(4,1)S(1)} %bitcast.159, bf16[4,256]{1,0:T(4,128)(2,1)S(1)} %slice.263, pred[4,1024]{1,0:T(4,128)(4,1)S(1)} %iota_compare_fusion.1), kind=kOutput, calls=%fused_computation.174 | convolution fusion | flops 4220920 | bytes 2136608 | tf_op jit(solution)/shard_map/rkf,rfh->rhk/dot_general | solution.py:105
  133.5 2.0 %fusion.14 = f32[4,2,256]{2,1,0:T(2,128)S(1)} fusion(bf16[8,2,1024,256]{3,2,1,0:T(8,128)(2,1)} %param.21, f32[4,2,1024]{2,1,0:T(2,128)S(1)} %get-tuple-element.75, pred[4,1024]{1,0:T(4,128)(4,1)S(1)} %iota_compare_fusion.1, f32[4,2]{1,0:T(4,128)S(1)} %get-tuple-element.74), kind=kOutput, calls=%fused_computation.19 | convolution fusion | flops 4218880 | bytes 2142240 | tf_op jit(solution)/shard_map/rhk,rkf->rhf/dot_general | solution.py:112
  136.7 5.7 %collective-permute-start.4 = (f32[4,2,130]{0,1,2:T(2,128)S(1)}, f32[4,2,130]{0,1,2:T(2,128)S(1)}, u32[]{:S(2)}, u32[]{:S(2)}) collective-permute-start(f32[4,2,130]{0,1,2:T(2,128)S(1)} %pad_maximum_fusion.7), channel_id=1, source_target_pairs={{8,0},{16,8},{24,16},{32,24},{40,32},{48,40},{56,48},{64,56},{72,6... | collective-permute-start | bytes 12488 | tf_op jit(solution)/shard_map/ppermute | solution.py:210
  142.8 0.8 copy.195
  143.6 1.4 collective-permute-done.2
  (121 shorter events, 9.4 us)
Async XLA Ops:
  7.2 30.2 %copy-start.9 = (f32[4096]{0:T(1024)S(1)}, f32[4096]{0:T(1024)}, u32[]{:S(2)}) copy-start(f32[4096]{0:T(1024)} %param.13) | copy-start | bytes 49156
  7.2 30.2 %copy-start.10 = (f32[4096]{0:T(1024)S(1)}, f32[4096]{0:T(1024)}, u32[]{:S(2)}) copy-start(f32[4096]{0:T(1024)} %param.14) | copy-start | bytes 49156
  7.2 90.8 %all-gather.2.cloned.1.call-start = ((), (), s32[]{:S(2)}) async-start(), calls=%async_computation | async-start | bytes 5283840 | tf_op jit(solution)/shard_map/all_gather | solution.py:161
  8.3 21.6 %collective-permute-start = (bf16[516,512]{1,0:T(8,128)(2,1)S(1)}, bf16[516,512]{1,0:T(8,128)(2,1)S(1)}, u32[]{:S(2)}, u32[]{:S(2)}) collective-permute-start(bf16[516,512]{1,0:T(8,128)(2,1)S(1)} %pad_maximum_fusion.3), channel_id=1, source_target_pairs={{0,1},{1,0},{2,3},{3,2},{4,5},{5,4},{6,7},{7,6},{8,9},{9,8},{10,11... | collective-permute-start | bytes 1585160 | tf_op jit(solution)/shard_map/ppermute | solution.py:159
  58.4 6.9 %copy-start.11 = (f32[3,256]{1,0:T(4,128)S(1)}, f32[3,256]{1,0:T(4,128)}, u32[]{:S(2)}) copy-start(f32[3,256]{1,0:T(4,128)} %param.16) | copy-start | bytes 9220
  58.4 7.6 %copy-start.8 = (s32[4,3]{1,0:T(4,128)S(1)}, s32[4,3]{1,0:T(4,128)}, u32[]{:S(2)}) copy-start(s32[4,3]{1,0:T(4,128)} %param.20) | copy-start | bytes 148
  58.4 9.3 %copy-start.4 = (bf16[1,2,512,256]{3,2,1,0:T(8,128)(2,1)S(1)}, bf16[1,2,512,256]{3,2,1,0:T(8,128)(2,1)}, u32[]{:S(2)}) copy-start(bf16[1,2,512,256]{3,2,1,0:T(8,128)(2,1)} %param.17) | copy-start | bytes 1572868
  65.2 5.6 %copy-start.2 = (bf16[4,2,256,256]{3,2,1,0:T(8,128)(2,1)S(1)}, bf16[4,2,256,256]{3,2,1,0:T(8,128)(2,1)}, u32[]{:S(2)}) copy-start(bf16[4,2,256,256]{3,2,1,0:T(8,128)(2,1)} %param.19) | copy-start | bytes 3145732
  98.0 6.8 %slice-start = ((s8[6291456]{0:T(1024)(128)(4,1)}), s8[4194304]{0:T(1024)(128)(4,1)S(1)}, s32[]{:S(2)}) async-start(s8[6291456]{0:T(1024)(128)(4,1)} %bitcast.139), calls=%async_computation.1 | async-start | bytes 8388608
  101.1 3.7 %slice-start.1 = ((s8[6291456]{0:T(1024)(128)(4,1)}), s8[2097152]{0:T(1024)(128)(4,1)S(1)}, s32[]{:S(2)}) async-start(s8[6291456]{0:T(1024)(128)(4,1)} %bitcast.139), calls=%async_computation.2 | async-start | bytes 4194304
  109.9 2.9 %copy-start = (f32[516,16]{1,0:T(8,128)S(1)}, f32[516,16]{1,0:T(8,128)}, u32[]{:S(2)}) copy-start(f32[516,16]{1,0:T(8,128)} %copy.166) | copy-start | bytes 99076
  112.8 8.6 %copy-start.1 = (bf16[512,2,128]{2,0,1:T(8,128)(2,1)S(1)}, bf16[512,2,128]{2,0,1:T(8,128)(2,1)}, u32[]{:S(2)}) copy-start(bf16[512,2,128]{2,0,1:T(8,128)(2,1)} %copy.169) | copy-start | bytes 786436
  113.6 8.5 %copy-start.3 = (pred[512,1024]{1,0:T(8,128)(4,1)S(1)}, pred[512,1024]{1,0:T(8,128)(4,1)}, u32[]{:S(2)}) copy-start(pred[512,1024]{1,0:T(8,128)(4,1)} %pad_add_fusion) | copy-start | bytes 1572868
  115.8 10.3 %collective-permute-start.1 = (f32[4,257]{1,0:T(4,128)S(1)}, f32[4,257]{1,0:T(4,128)S(1)}, u32[]{:S(2)}, u32[]{:S(2)}) collective-permute-start(f32[4,257]{1,0:T(4,128)S(1)} %get-tuple-element.65), channel_id=1, source_target_pairs={{8,0},{16,8},{24,16},{32,24},{40,32},{48,40},{56,48},{64,56},{72,6... | collective-permute-start | bytes 12344 | tf_op jit(solution)/shard_map/ppermute | solution.py:201
  121.1 9.9 %collective-permute-start.3 = (f32[4,257]{1,0:T(4,128)S(1)}, f32[4,257]{1,0:T(4,128)S(1)}, u32[]{:S(2)}, u32[]{:S(2)}) collective-permute-start(f32[4,257]{1,0:T(4,128)S(1)} %get-tuple-element.66), channel_id=1, source_target_pairs={{0,8},{8,16},{16,24},{24,32},{32,40},{40,48},{48,56},{56,64},{64,7... | collective-permute-start | bytes 12344 | tf_op jit(solution)/shard_map/ppermute | solution.py:201
  122.1 2.4 %copy-start.7 = (bf16[1,1,512,256]{2,3,1,0:T(8,128)(2,1)S(1)}, bf16[1,1,512,256]{2,3,1,0:T(8,128)(2,1)}, u32[]{:S(2)}) copy-start(bf16[1,1,512,256]{2,3,1,0:T(8,128)(2,1)} %copy.160) | copy-start | bytes 786436
  124.5 1.0 copy-start.6
  124.5 1.4 copy-start.5
  136.3 8.7 %collective-permute-start.2 = (f32[4,2,130]{0,1,2:T(2,128)S(1)}, f32[4,2,130]{0,1,2:T(2,128)S(1)}, u32[]{:S(2)}, u32[]{:S(2)}) collective-permute-start(f32[4,2,130]{0,1,2:T(2,128)S(1)} %pad_maximum_fusion.6), channel_id=1, source_target_pairs={{0,8},{8,16},{16,24},{24,32},{32,40},{40,48},{48,56},{56,64},{64,7... | collective-permute-start | bytes 12488 | tf_op jit(solution)/shard_map/ppermute | solution.py:210
  136.7 8.3 %collective-permute-start.4 = (f32[4,2,130]{0,1,2:T(2,128)S(1)}, f32[4,2,130]{0,1,2:T(2,128)S(1)}, u32[]{:S(2)}, u32[]{:S(2)}) collective-permute-start(f32[4,2,130]{0,1,2:T(2,128)S(1)} %pad_maximum_fusion.7), channel_id=1, source_target_pairs={{8,0},{16,8},{24,16},{32,24},{40,32},{48,40},{56,48},{64,56},{72,6... | collective-permute-start | bytes 12488 | tf_op jit(solution)/shard_map/ppermute | solution.py:210
Sparse Core Ops, SparseCore 0:
  37.5 60.5 all-gather.1
